TPU v7x, 1024 devices: a whole 4x8x16 slice. The times are simulated.
1024 devices in a mesh: row: 16 (over z), col: 64 (over x, y, core).
Axes of the slice: x: 4, y: 8, z: 16, core: 2. Of those that a mesh axis runs over, the one named last changes fastest.
Arguments:
- gradient: float32 [5120, 16384], P('row', 'col'), may hold values from -6 to 6
- eigenbasis: bfloat16 [5120, 5120], P(None, 'row'), may hold values from -0.078125 to 0.078125
- first_moment: float32 [5120, 16384], P('row', 'col'), may hold values from -3 to 3
- second_moment: float32 [5120, 16384], P('row', 'col'), may hold values from 0.05 to 4
Outputs:
- new_first: float32 [5120, 16384], P('row', 'col')
- new_second: float32 [5120, 16384], P('row', 'col')
- direction: float32 [5120, 16384], P('row', 'col')
All inputs are finite; a program needn't handle non-finite values.
Results may differ from a plain program's by a relative error of at most 0.003.
Values may be sent and summed in bfloat16 or wider, within the bound.
No kernel may reach another device: no remote copies, remote signals or barrier semaphores. Data moves between devices by JAX's collectives and lax.ppermute only.
A program may use at most 64 MiB of HBM per device.

v0:
```python
import jax
import jax.numpy as jnp
from jax import lax
from jax.sharding import PartitionSpec as P

STEP = 2


def moments(rotated, first_moment, second_moment):
    new_first = 0.9 * first_moment + 0.1 * rotated
    new_second = 0.99 * second_moment + 0.01 * rotated * rotated
    fix_first = 1.0 - 0.9**STEP
    fix_second = 1.0 - 0.99**STEP
    step_low = (new_first / fix_first / (jnp.sqrt(new_second / fix_second) + 1e-08)).astype(
        jnp.bfloat16
    )
    return (new_first, new_second, step_low)


def local(gradient, eigenbasis, first_moment, second_moment):
    grad_low = gradient.astype(jnp.bfloat16)
    grad_whole = lax.all_gather(grad_low, "row", axis=0, tiled=True)
    rotated = lax.dot_general(
        eigenbasis, grad_whole, (((0,), (0,)), ((), ())), preferred_element_type=jnp.float32
    )
    new_first, new_second, step_low = moments(rotated, first_moment, second_moment)
    terms = jnp.dot(eigenbasis, step_low, preferred_element_type=jnp.float32)
    direction = lax.psum_scatter(terms, "row", scatter_dimension=0, tiled=True)
    return (new_first, new_second, direction)


def solution(mesh):
    in_specs = (P("row", "col"), P(None, "row"), P("row", "col"), P("row", "col"))
    out_specs = (P("row", "col"), P("row", "col"), P("row", "col"))
    return jax.shard_map(local, mesh=mesh, in_specs=in_specs, out_specs=out_specs, check_vma=False)
```

profile of v0, /device:TPU:6, one launch (start us, length us, event | category | flops | bytes accessed | tf_op | source)
XLA Modules:
  0.0 201.5 jit_solution(10180756713854865154)
XLA Ops:
  7.2 0.0 copy-start
  7.2 0.0 all-gather.2.cloned.1.call-start
  7.2 1.8 convert_element_type.6
  9.0 0.0 all-gather.2.cloned.1.call-update
  9.1 0.0 reduce-scatter.4.cloned.1.call-start
  9.1 88.4 %all-gather.2.cloned.1.call-done = bf16[5120,256]{1,0:T(8,128)(2,1)} async-done(((bf16[320,256]{1,0:T(8,128)(2,1)}), bf16[5120,256]{1,0:T(8,128)(2,1)}) %all-gather.2.cloned.1.call-update) | async-done | bytes 2621456 | tf_op jit(solution)/shard_map/all_gather | solution.py:22
  97.5 0.0 copy-done
  97.5 2.9 %fusion = (f32[320,256]{1,0:T(8,128)S(1)}, f32[320,256]{1,0:T(8,128)S(1)}) fusion(f32[320,256]{1,0:T(8,128)} %param.7, f32[320,256]{1,0:T(8,128)} %param.6, bf16[5120,320]{0,1:T(8,128)(2,1)S(1)} %copy-done, bf16[5120,256]{1,0:T(8,128)(2,1)} %all-gather.2.cloned.1.call-done), kind=kOutput, calls=%fused_computation.2 | convolution fusion | flops 839434240 | bytes 7208960 | tf_op jit(solution)/shard_map/dot_general | solution.py:23
  100.4 0.0 copy-start.1
  100.4 0.0 copy-start.2
  100.4 0.7 copy-done.1
  101.1 0.1 copy-done.2
  101.3 3.9 %convolution_bitcast_fusion = f32[5120,256]{0,1:T(8,128)} fusion(bf16[5120,320]{0,1:T(8,128)(2,1)S(1)} %copy-done, f32[320,256]{1,0:T(8,128)S(1)} %get-tuple-element.9, f32[320,256]{1,0:T(8,128)S(1)} %get-tuple-element.10), kind=kOutput, calls=%fused_computation | convolution fusion | flops 839270400 | bytes 9175040 | tf_op jit(solution)/shard_map/dot_general | solution.py:27
  105.2 5.9 %copy.9 = f32[5120,256]{1,0:T(8,128)} copy(f32[5120,256]{0,1:T(8,128)} %convolution_bitcast_fusion) | data formatting | bytes 10485760
  111.1 0.0 reduce-scatter.4.cloned.1.call-update
  111.2 83.5 %reduce-scatter.4.cloned.1.call-done = f32[320,256]{1,0:T(8,128)} async-done(((f32[5120,256]{1,0:T(8,128)}), f32[320,256]{1,0:T(8,128)}) %reduce-scatter.4.cloned.1.call-update) | async-done | bytes 327696
Async XLA Ops:
  7.2 90.4 %copy-start = (bf16[5120,320]{0,1:T(8,128)(2,1)S(1)}, bf16[5120,320]{0,1:T(8,128)(2,1)}, u32[]{:S(2)}) copy-start(bf16[5120,320]{0,1:T(8,128)(2,1)} %param.5) | copy-start | bytes 9830404
  7.2 90.4 %all-gather.2.cloned.1.call-start = ((), (), s32[]{:S(2)}) async-start(), calls=%async_computation.1 | async-start | bytes 2785280 | tf_op jit(solution)/shard_map/all_gather | solution.py:22
  9.1 185.6 %reduce-scatter.4.cloned.1.call-start = ((), (), s32[]{:S(2)}) async-start(), calls=%async_computation.2 | async-start | bytes 5570560
  100.4 0.7 copy-start.1
  100.4 0.8 copy-start.2
Sparse Core Ops, SparseCore 0:
  11.2 86.2 all-gather.1
  111.3 83.3 reduce-scatter.3
where the time goes:
time: 202 us
  waiting for transfers between devices  172 us (85%)
  between operations  14.1 us (7%)
  matrix products  6.82 us (3%)
  local copies, waits for them, and re-layouts  6.76 us (3%)
    all_gather x1, waiting for transfers between devices, local(): grad_whole = lax.all_gather(grad_low, 'row', axis=0, tiled=True)  88.4 us
    unnamed x3, waiting for transfers between devices  83.6 us
    unnamed x7, local copies, waits for them, and re-layouts  6.76 us
  transfers between devices with their start and end apart: 2, of which 2 were waited for; matrix products, arithmetic and copies ran while one was open for 0% of the time, Pallas kernels for 0%

commit v1 on v0

--- a/solution.py
+++ b/solution.py
@@ -17,9 +17,28 @@
     return (new_first, new_second, step_low)
 
 
+def ring_gather(x, n):
+    i = lax.axis_index("row")
+    b = x.shape[0]
+    out = jnp.zeros((n * b,) + x.shape[1:], x.dtype)
+    out = lax.dynamic_update_slice_in_dim(out, x, i * b, axis=0)
+    fwd = [(j, (j + 1) % n) for j in range(n)]
+    bwd = [(j, (j - 1) % n) for j in range(n)]
+    a = x
+    c = x
+    for s in range(1, n // 2 + 1):
+        a = lax.ppermute(a, "row", fwd)
+        out = lax.dynamic_update_slice_in_dim(out, a, ((i - s) % n) * b, axis=0)
+        if s < n - s:
+            c = lax.ppermute(c, "row", bwd)
+            out = lax.dynamic_update_slice_in_dim(out, c, ((i + s) % n) * b, axis=0)
+    return out
+
+
 def local(gradient, eigenbasis, first_moment, second_moment):
+    n = lax.axis_size("row")
     grad_low = gradient.astype(jnp.bfloat16)
-    grad_whole = lax.all_gather(grad_low, "row", axis=0, tiled=True)
+    grad_whole = ring_gather(grad_low, n)
     rotated = lax.dot_general(
         eigenbasis, grad_whole, (((0,), (0,)), ((), ())), preferred_element_type=jnp.float32
     )

time: 202 us -> 196 us (0.970)
  waiting for transfers between devices: 172 us -> 88.7 us
  starting transfers between devices: 0.08 us -> 64.3 us
  local copies, waits for them, and re-layouts: 6.76 us -> 19.5 us
    all_gather x1 -> x0, waiting for transfers between devices: 88.4 us -> none  [local(): grad_whole = lax.all_gather(grad_low, 'row', axis=0, tiled=True)]
    ppermute x0 -> x15, starting transfers between devices: none -> 64.3 us  [the longest x7 46.7 us: ring_gather(): c = lax.ppermute(c, 'row', bwd)]
    dynamic_update_slice x0 -> x15, local copies, waits for them, and re-layouts: none -> 11 us  [the longest x8 6.35 us: ring_gather(): out = lax.dynamic_update_slice_in_dim(out, a, (i - s) % n * b, axis=0)]
    ppermute x0 -> x15, waiting for transfers between devices: none -> 7.44 us  [the longest x8 7.42 us: ring_gather(): a = lax.ppermute(a, 'row', fwd)]
    unnamed x3 -> x2, waiting for transfers between devices: 83.6 us -> 81.2 us
    unnamed x7 -> x13, local copies, waits for them, and re-layouts: 6.76 us -> 6.83 us
  transfers between devices with their start and end apart: 2 -> 16, of which waited for: 2 -> 3; matrix products, arithmetic and copies ran while one was open for 0% -> 5% of each run, Pallas kernels for 0% -> 0%
where the time goes in v1:
time: 196 us; the launch traced here: 195 us
  waiting for transfers between devices  88.7 us (45%)
  starting transfers between devices  64.3 us (33%)
  local copies, waits for them, and re-layouts  19.5 us (10%)
  between operations  14.6 us (7%)
  matrix products  6.73 us (3%)
    unnamed x2, waiting for transfers between devices  81.2 us
    ppermute x7, starting transfers between devices, ring_gather(): c = lax.ppermute(c, 'row', bwd)  46.7 us
    ppermute x8, starting transfers between devices, ring_gather(): a = lax.ppermute(a, 'row', fwd)  17.6 us
    ppermute x8, waiting for transfers between devices, ring_gather(): a = lax.ppermute(a, 'row', fwd)  7.42 us
    unnamed x13, local copies, waits for them, and re-layouts  6.83 us
    dynamic_update_slice x8, local copies, waits for them, and re-layouts, ring_gather(): out = lax.dynamic_update_slice_in_dim(out, a, (i - s) % n * b, axis=0)  6.35 us
    dynamic_update_slice x7, local copies, waits for them, and re-layouts, ring_gather(): out = lax.dynamic_update_slice_in_dim(out, c, (i + s) % n * b, axis=0)  4.7 us
    dot_general x1, matrix products, local(): terms = jnp.dot(eigenbasis, step_low, preferred_element_type=jnp.float32)  3.97 us
  transfers between devices with their start and end apart: 16, of which 3 were waited for; matrix products, arithmetic and copies ran while one was open for 5% of the time, Pallas kernels for 0%

profile of v1, /device:TPU:6, one launch (start us, length us, event | category | flops | bytes accessed | tf_op | source)
XLA Modules:
  0.0 194.6 jit_solution(5477032165371363884)
XLA Ops:
  7.2 1.7 broadcast_in_dim.3
  8.9 0.7 constant_dynamic-update-slice_fusion.15
  9.6 4.3 %collective-permute-start = (bf16[320,256]{1,0:T(8,128)(2,1)}, bf16[320,256]{1,0:T(8,128)(2,1)}, u32[]{:S(2)}, u32[]{:S(2)}) collective-permute-start(bf16[320,256]{1,0:T(8,128)(2,1)} %get-tuple-element.10), channel_id=1, source_target_pairs={{0,64},{64,128},{128,192},{192,256},{256,320},{320,384},{384,448},... | collective-permute-start | bytes 491528 | tf_op jit(solution)/shard_map/ppermute | solution.py:30
  13.9 15.9 %collective-permute-start.1 = (bf16[320,256]{1,0:T(8,128)(2,1)}, bf16[320,256]{1,0:T(8,128)(2,1)S(1)}, u32[]{:S(2)}, u32[]{:S(2)}) collective-permute-start(bf16[320,256]{1,0:T(8,128)(2,1)} %get-tuple-element.10), channel_id=1, source_target_pairs={{0,960},{64,0},{128,64},{192,128},{256,192},{320,256},{384,320},{4... | collective-permute-start | bytes 491528 | tf_op jit(solution)/shard_map/ppermute | solution.py:33
  30.1 2.3 %collective-permute-done = bf16[320,256]{1,0:T(8,128)(2,1)} collective-permute-done((bf16[320,256]{1,0:T(8,128)(2,1)}, bf16[320,256]{1,0:T(8,128)(2,1)}, u32[]{:S(2)}, u32[]{:S(2)}) %collective-permute-start) | collective-permute-done | bytes 163872 | tf_op jit(solution)/shard_map/ppermute | solution.py:30
  32.4 1.9 collective-permute-start.2
  34.3 5.1 %collective-permute-start.3 = (bf16[320,256]{1,0:T(8,128)(2,1)S(1)}, bf16[320,256]{1,0:T(8,128)(2,1)S(1)}, u32[]{:S(2)}, u32[]{:S(2)}) collective-permute-start(bf16[320,256]{1,0:T(8,128)(2,1)S(1)} %collective-permute-done.1), channel_id=1, source_target_pairs={{0,960},{64,0},{128,64},{192,128},{256,192},{320,256},{384,320},{4... | collective-permute-start | bytes 491528 | tf_op jit(solution)/shard_map/ppermute | solution.py:33
  39.4 1.6 constant_dynamic-update-slice_fusion.14
  41.7 1.9 collective-permute-start.4
  43.6 5.1 %collective-permute-start.5 = (bf16[320,256]{1,0:T(8,128)(2,1)S(1)}, bf16[320,256]{1,0:T(8,128)(2,1)S(1)}, u32[]{:S(2)}, u32[]{:S(2)}) collective-permute-start(bf16[320,256]{1,0:T(8,128)(2,1)S(1)} %collective-permute-done.3), channel_id=1, source_target_pairs={{0,960},{64,0},{128,64},{192,128},{256,192},{320,256},{384,320},{4... | collective-permute-start | bytes 491528 | tf_op jit(solution)/shard_map/ppermute | solution.py:33
  48.8 0.7 constant_dynamic-update-slice_fusion.12
  50.1 1.9 collective-permute-start.6
  52.0 5.1 %collective-permute-start.7 = (bf16[320,256]{1,0:T(8,128)(2,1)S(1)}, bf16[320,256]{1,0:T(8,128)(2,1)S(1)}, u32[]{:S(2)}, u32[]{:S(2)}) collective-permute-start(bf16[320,256]{1,0:T(8,128)(2,1)S(1)} %collective-permute-done.5), channel_id=1, source_target_pairs={{0,960},{64,0},{128,64},{192,128},{256,192},{320,256},{384,320},{4... | collective-permute-start | bytes 491528 | tf_op jit(solution)/shard_map/ppermute | solution.py:33
  57.2 0.7 constant_dynamic-update-slice_fusion.10
  57.9 0.7 constant_dynamic-update-slice_fusion.9
  58.5 1.9 collective-permute-start.8
  60.5 5.1 %collective-permute-start.9 = (bf16[320,256]{1,0:T(8,128)(2,1)S(1)}, bf16[320,256]{1,0:T(8,128)(2,1)S(1)}, u32[]{:S(2)}, u32[]{:S(2)}) collective-permute-start(bf16[320,256]{1,0:T(8,128)(2,1)S(1)} %collective-permute-done.7), channel_id=1, source_target_pairs={{0,960},{64,0},{128,64},{192,128},{256,192},{320,256},{384,320},{4... | collective-permute-start | bytes 491528 | tf_op jit(solution)/shard_map/ppermute | solution.py:33
  67.0 1.9 collective-permute-start.10
  68.9 5.1 %collective-permute-start.11 = (bf16[320,256]{1,0:T(8,128)(2,1)S(1)}, bf16[320,256]{1,0:T(8,128)(2,1)S(1)}, u32[]{:S(2)}, u32[]{:S(2)}) collective-permute-start(bf16[320,256]{1,0:T(8,128)(2,1)S(1)} %collective-permute-done.9), channel_id=1, source_target_pairs={{0,960},{64,0},{128,64},{192,128},{256,192},{320,256},{384,320},{4... | collective-permute-start | bytes 491528 | tf_op jit(solution)/shard_map/ppermute | solution.py:33
  74.0 0.7 constant_dynamic-update-slice_fusion.6
  75.4 1.9 collective-permute-start.12
  77.3 5.1 %collective-permute-start.13 = (bf16[320,256]{1,0:T(8,128)(2,1)S(1)}, bf16[320,256]{1,0:T(8,128)(2,1)S(1)}, u32[]{:S(2)}, u32[]{:S(2)}) collective-permute-start(bf16[320,256]{1,0:T(8,128)(2,1)S(1)} %collective-permute-done.11), channel_id=1, source_target_pairs={{0,960},{64,0},{128,64},{192,128},{256,192},{320,256},{384,320},{4... | collective-permute-start | bytes 491528 | tf_op jit(solution)/shard_map/ppermute | solution.py:33
  82.5 0.7 constant_dynamic-update-slice_fusion.4
  83.1 0.7 constant_dynamic-update-slice_fusion.3
  83.8 1.9 collective-permute-start.14
  85.7 0.7 constant_dynamic-update-slice_fusion.2
  87.1 5.1 %collective-permute-done.14 = bf16[320,256]{1,0:T(8,128)(2,1)S(1)} collective-permute-done((bf16[320,256]{1,0:T(8,128)(2,1)S(1)}, bf16[320,256]{1,0:T(8,128)(2,1)S(1)}, u32[]{:S(2)}, u32[]{:S(2)}) %collective-permute-start.14) | collective-permute-done | bytes 163872 | tf_op jit(solution)/shard_map/ppermute | solution.py:30
  92.9 2.8 %fusion = (f32[320,256]{1,0:T(8,128)S(1)}, f32[320,256]{1,0:T(8,128)S(1)}) fusion(f32[320,256]{1,0:T(8,128)S(1)} %copy-done.4, f32[320,256]{1,0:T(8,128)S(1)} %copy-done.5, bf16[5120,320]{0,1:T(8,128)(2,1)S(1)} %copy-done, bf16[5120,256]{1,0:T(8,128)(2,1)} %constant_dynamic-update-slice_fusion), kind=kOutput, calls=%fused_computation.3 | convolution fusion | flops 839434240 | bytes 7208960 | tf_op jit(solution)/shard_map/dot_general | solution.py:42
  95.7 0.7 copy-done.1
  96.5 4.0 %convolution_bitcast_fusion = f32[5120,256]{0,1:T(8,128)} fusion(bf16[5120,320]{0,1:T(8,128)(2,1)S(1)} %copy-done, f32[320,256]{1,0:T(8,128)S(1)} %get-tuple-element.11, f32[320,256]{1,0:T(8,128)S(1)} %get-tuple-element.12), kind=kOutput, calls=%fused_computation | convolution fusion | flops 839270400 | bytes 9175040 | tf_op jit(solution)/shard_map/dot_general | solution.py:46
  100.5 6.0 %copy.9 = f32[5120,256]{1,0:T(8,128)} copy(f32[5120,256]{0,1:T(8,128)} %convolution_bitcast_fusion) | data formatting | bytes 10485760
  106.5 81.2 %reduce-scatter.4.cloned.1.call-done = f32[320,256]{1,0:T(8,128)} async-done(((f32[5120,256]{1,0:T(8,128)}), f32[320,256]{1,0:T(8,128)}) %reduce-scatter.4.cloned.1.call-update) | async-done | bytes 327696
  (33 shorter events, 4.9 us)
Async XLA Ops:
  7.2 85.8 %copy-start = (bf16[5120,320]{0,1:T(8,128)(2,1)S(1)}, bf16[5120,320]{0,1:T(8,128)(2,1)}, u32[]{:S(2)}) copy-start(bf16[5120,320]{0,1:T(8,128)(2,1)} %param.5) | copy-start | bytes 9830404
  7.2 180.6 %reduce-scatter.4.cloned.1.call-start = ((), (), s32[]{:S(2)}) async-start(), calls=%async_computation.1 | async-start | bytes 5570560
  7.2 1.7 copy-start.3
  9.6 22.7 %collective-permute-start = (bf16[320,256]{1,0:T(8,128)(2,1)}, bf16[320,256]{1,0:T(8,128)(2,1)}, u32[]{:S(2)}, u32[]{:S(2)}) collective-permute-start(bf16[320,256]{1,0:T(8,128)(2,1)} %get-tuple-element.10), channel_id=1, source_target_pairs={{0,64},{64,128},{128,192},{192,256},{256,320},{320,384},{384,448},... | collective-permute-start | bytes 491528 | tf_op jit(solution)/shard_map/ppermute | solution.py:30
  13.9 20.4 %collective-permute-start.1 = (bf16[320,256]{1,0:T(8,128)(2,1)}, bf16[320,256]{1,0:T(8,128)(2,1)S(1)}, u32[]{:S(2)}, u32[]{:S(2)}) collective-permute-start(bf16[320,256]{1,0:T(8,128)(2,1)} %get-tuple-element.10), channel_id=1, source_target_pairs={{0,960},{64,0},{128,64},{192,128},{256,192},{320,256},{384,320},{4... | collective-permute-start | bytes 491528 | tf_op jit(solution)/shard_map/ppermute | solution.py:33
  30.1 62.8 %copy-start.4 = (f32[320,256]{1,0:T(8,128)S(1)}, f32[320,256]{1,0:T(8,128)}, u32[]{:S(2)}) copy-start(f32[320,256]{1,0:T(8,128)} %param.7) | copy-start | bytes 983044
  30.1 62.8 %copy-start.5 = (f32[320,256]{1,0:T(8,128)S(1)}, f32[320,256]{1,0:T(8,128)}, u32[]{:S(2)}) copy-start(f32[320,256]{1,0:T(8,128)} %param.6) | copy-start | bytes 983044
  32.4 9.3 %collective-permute-start.2 = (bf16[320,256]{1,0:T(8,128)(2,1)}, bf16[320,256]{1,0:T(8,128)(2,1)S(1)}, u32[]{:S(2)}, u32[]{:S(2)}) collective-permute-start(bf16[320,256]{1,0:T(8,128)(2,1)} %collective-permute-done), channel_id=1, source_target_pairs={{0,64},{64,128},{128,192},{192,256},{256,320},{320,384},{384,448},... | collective-permute-start | bytes 491528 | tf_op jit(solution)/shard_map/ppermute | solution.py:30
  34.3 9.3 %collective-permute-start.3 = (bf16[320,256]{1,0:T(8,128)(2,1)S(1)}, bf16[320,256]{1,0:T(8,128)(2,1)S(1)}, u32[]{:S(2)}, u32[]{:S(2)}) collective-permute-start(bf16[320,256]{1,0:T(8,128)(2,1)S(1)} %collective-permute-done.1), channel_id=1, source_target_pairs={{0,960},{64,0},{128,64},{192,128},{256,192},{320,256},{384,320},{4... | collective-permute-start | bytes 491528 | tf_op jit(solution)/shard_map/ppermute | solution.py:33
  41.7 8.4 %collective-permute-start.4 = (bf16[320,256]{1,0:T(8,128)(2,1)S(1)}, bf16[320,256]{1,0:T(8,128)(2,1)S(1)}, u32[]{:S(2)}, u32[]{:S(2)}) collective-permute-start(bf16[320,256]{1,0:T(8,128)(2,1)S(1)} %collective-permute-done.2), channel_id=1, source_target_pairs={{0,64},{64,128},{128,192},{192,256},{256,320},{320,384},{384,448},... | collective-permute-start | bytes 491528 | tf_op jit(solution)/shard_map/ppermute | solution.py:30
  43.6 8.4 %collective-permute-start.5 = (bf16[320,256]{1,0:T(8,128)(2,1)S(1)}, bf16[320,256]{1,0:T(8,128)(2,1)S(1)}, u32[]{:S(2)}, u32[]{:S(2)}) collective-permute-start(bf16[320,256]{1,0:T(8,128)(2,1)S(1)} %collective-permute-done.3), channel_id=1, source_target_pairs={{0,960},{64,0},{128,64},{192,128},{256,192},{320,256},{384,320},{4... | collective-permute-start | bytes 491528 | tf_op jit(solution)/shard_map/ppermute | solution.py:33
  50.1 8.4 %collective-permute-start.6 = (bf16[320,256]{1,0:T(8,128)(2,1)S(1)}, bf16[320,256]{1,0:T(8,128)(2,1)S(1)}, u32[]{:S(2)}, u32[]{:S(2)}) collective-permute-start(bf16[320,256]{1,0:T(8,128)(2,1)S(1)} %collective-permute-done.4), channel_id=1, source_target_pairs={{0,64},{64,128},{128,192},{192,256},{256,320},{320,384},{384,448},... | collective-permute-start | bytes 491528 | tf_op jit(solution)/shard_map/ppermute | solution.py:30
  52.0 8.4 %collective-permute-start.7 = (bf16[320,256]{1,0:T(8,128)(2,1)S(1)}, bf16[320,256]{1,0:T(8,128)(2,1)S(1)}, u32[]{:S(2)}, u32[]{:S(2)}) collective-permute-start(bf16[320,256]{1,0:T(8,128)(2,1)S(1)} %collective-permute-done.5), channel_id=1, source_target_pairs={{0,960},{64,0},{128,64},{192,128},{256,192},{320,256},{384,320},{4... | collective-permute-start | bytes 491528 | tf_op jit(solution)/shard_map/ppermute | solution.py:33
  58.5 8.4 %collective-permute-start.8 = (bf16[320,256]{1,0:T(8,128)(2,1)S(1)}, bf16[320,256]{1,0:T(8,128)(2,1)S(1)}, u32[]{:S(2)}, u32[]{:S(2)}) collective-permute-start(bf16[320,256]{1,0:T(8,128)(2,1)S(1)} %collective-permute-done.6), channel_id=1, source_target_pairs={{0,64},{64,128},{128,192},{192,256},{256,320},{320,384},{384,448},... | collective-permute-start | bytes 491528 | tf_op jit(solution)/shard_map/ppermute | solution.py:30
  60.5 8.4 %collective-permute-start.9 = (bf16[320,256]{1,0:T(8,128)(2,1)S(1)}, bf16[320,256]{1,0:T(8,128)(2,1)S(1)}, u32[]{:S(2)}, u32[]{:S(2)}) collective-permute-start(bf16[320,256]{1,0:T(8,128)(2,1)S(1)} %collective-permute-done.7), channel_id=1, source_target_pairs={{0,960},{64,0},{128,64},{192,128},{256,192},{320,256},{384,320},{4... | collective-permute-start | bytes 491528 | tf_op jit(solution)/shard_map/ppermute | solution.py:33
  67.0 8.4 %collective-permute-start.10 = (bf16[320,256]{1,0:T(8,128)(2,1)S(1)}, bf16[320,256]{1,0:T(8,128)(2,1)S(1)}, u32[]{:S(2)}, u32[]{:S(2)}) collective-permute-start(bf16[320,256]{1,0:T(8,128)(2,1)S(1)} %collective-permute-done.8), channel_id=1, source_target_pairs={{0,64},{64,128},{128,192},{192,256},{256,320},{320,384},{384,448},... | collective-permute-start | bytes 491528 | tf_op jit(solution)/shard_map/ppermute | solution.py:30
  68.9 8.4 %collective-permute-start.11 = (bf16[320,256]{1,0:T(8,128)(2,1)S(1)}, bf16[320,256]{1,0:T(8,128)(2,1)S(1)}, u32[]{:S(2)}, u32[]{:S(2)}) collective-permute-start(bf16[320,256]{1,0:T(8,128)(2,1)S(1)} %collective-permute-done.9), channel_id=1, source_target_pairs={{0,960},{64,0},{128,64},{192,128},{256,192},{320,256},{384,320},{4... | collective-permute-start | bytes 491528 | tf_op jit(solution)/shard_map/ppermute | solution.py:33
  75.4 8.4 %collective-permute-start.12 = (bf16[320,256]{1,0:T(8,128)(2,1)S(1)}, bf16[320,256]{1,0:T(8,128)(2,1)S(1)}, u32[]{:S(2)}, u32[]{:S(2)}) collective-permute-start(bf16[320,256]{1,0:T(8,128)(2,1)S(1)} %collective-permute-done.10), channel_id=1, source_target_pairs={{0,64},{64,128},{128,192},{192,256},{256,320},{320,384},{384,448},... | collective-permute-start | bytes 491528 | tf_op jit(solution)/shard_map/ppermute | solution.py:30
  77.3 9.1 %collective-permute-start.13 = (bf16[320,256]{1,0:T(8,128)(2,1)S(1)}, bf16[320,256]{1,0:T(8,128)(2,1)S(1)}, u32[]{:S(2)}, u32[]{:S(2)}) collective-permute-start(bf16[320,256]{1,0:T(8,128)(2,1)S(1)} %collective-permute-done.11), channel_id=1, source_target_pairs={{0,960},{64,0},{128,64},{192,128},{256,192},{320,256},{384,320},{4... | collective-permute-start | bytes 491528 | tf_op jit(solution)/shard_map/ppermute | solution.py:33
  83.8 8.4 %collective-permute-start.14 = (bf16[320,256]{1,0:T(8,128)(2,1)S(1)}, bf16[320,256]{1,0:T(8,128)(2,1)S(1)}, u32[]{:S(2)}, u32[]{:S(2)}) collective-permute-start(bf16[320,256]{1,0:T(8,128)(2,1)S(1)} %collective-permute-done.12), channel_id=1, source_target_pairs={{0,64},{64,128},{128,192},{192,256},{256,320},{320,384},{384,448},... | collective-permute-start | bytes 491528 | tf_op jit(solution)/shard_map/ppermute | solution.py:30
  95.7 0.7 copy-start.1
  95.7 0.8 copy-start.2
Sparse Core Ops, SparseCore 0:
  106.6 81.0 reduce-scatter.3

commit v2 on v1

--- a/solution.py
+++ b/solution.py
@@ -43,8 +43,10 @@
         eigenbasis, grad_whole, (((0,), (0,)), ((), ())), preferred_element_type=jnp.float32
     )
     new_first, new_second, step_low = moments(rotated, first_moment, second_moment)
-    terms = jnp.dot(eigenbasis, step_low, preferred_element_type=jnp.float32)
-    direction = lax.psum_scatter(terms, "row", scatter_dimension=0, tiled=True)
+    terms_t = lax.dot_general(
+        step_low, eigenbasis, (((0,), (1,)), ((), ())), preferred_element_type=jnp.float32
+    )
+    direction = lax.psum_scatter(terms_t, "row", scatter_dimension=1, tiled=True).T
     return (new_first, new_second, direction)
 
 

time: 196 us -> 190 us (0.969)
  local copies, waits for them, and re-layouts: 19.5 us -> 13.6 us
    reduce_scatter x0 -> x1, waiting for transfers between devices: none -> 81.5 us  [local(): lax.psum_scatter(terms_t, 'row', scatter_dimension=1, tiled=True)]
    unnamed x2 -> x1, waiting for transfers between devices: 81.2 us -> 0.02 us
    unnamed x13 -> x12, local copies, waits for them, and re-layouts: 6.83 us -> 0.84 us
where the time goes in v2:
time: 190 us; the launch traced here: 189 us
  waiting for transfers between devices  89 us (47%)
  starting transfers between devices  64.3 us (34%)
  between operations  14.5 us (8%)
  local copies, waits for them, and re-layouts  13.6 us (7%)
  matrix products  7 us (4%)
    reduce_scatter x1, waiting for transfers between devices, local(): lax.psum_scatter(terms_t, 'row', scatter_dimension=1, tiled=True)  81.5 us
    ppermute x7, starting transfers between devices, ring_gather(): c = lax.ppermute(c, 'row', bwd)  46.7 us
    ppermute x8, starting transfers between devices, ring_gather(): a = lax.ppermute(a, 'row', fwd)  17.6 us
    ppermute x8, waiting for transfers between devices, ring_gather(): a = lax.ppermute(a, 'row', fwd)  7.43 us
    dynamic_update_slice x8, local copies, waits for them, and re-layouts, ring_gather(): out = lax.dynamic_update_slice_in_dim(out, a, (i - s) % n * b, axis=0)  6.35 us
    dynamic_update_slice x7, local copies, waits for them, and re-layouts, ring_gather(): out = lax.dynamic_update_slice_in_dim(out, c, (i + s) % n * b, axis=0)  4.7 us
    dot_general x1, matrix products, local(): lax.dot_general(step_low, eigenbasis, (((0,), (1,)), ((), ())), preferred...  4.24 us
  transfers between devices with their start and end apart: 16, of which 3 were waited for; matrix products, arithmetic and copies ran while one was open for 5% of the time, Pallas kernels for 0%

profile of v2, /device:TPU:6, one launch (start us, length us, event | category | flops | bytes accessed | tf_op | source)
XLA Modules:
  0.0 189.2 jit_solution(12490558791588589459)
XLA Ops:
  7.2 1.7 broadcast_in_dim.3
  8.9 0.7 constant_dynamic-update-slice_fusion.15
  9.6 4.3 %collective-permute-start = (bf16[320,256]{1,0:T(8,128)(2,1)}, bf16[320,256]{1,0:T(8,128)(2,1)}, u32[]{:S(2)}, u32[]{:S(2)}) collective-permute-start(bf16[320,256]{1,0:T(8,128)(2,1)} %get-tuple-element.4), channel_id=1, source_target_pairs={{0,64},{64,128},{128,192},{192,256},{256,320},{320,384},{384,448},... | collective-permute-start | bytes 491528 | tf_op jit(solution)/shard_map/ppermute | solution.py:30
  13.9 15.9 %collective-permute-start.1 = (bf16[320,256]{1,0:T(8,128)(2,1)}, bf16[320,256]{1,0:T(8,128)(2,1)S(1)}, u32[]{:S(2)}, u32[]{:S(2)}) collective-permute-start(bf16[320,256]{1,0:T(8,128)(2,1)} %get-tuple-element.4), channel_id=1, source_target_pairs={{0,960},{64,0},{128,64},{192,128},{256,192},{320,256},{384,320},{4... | collective-permute-start | bytes 491528 | tf_op jit(solution)/shard_map/ppermute | solution.py:33
  30.1 2.3 %collective-permute-done = bf16[320,256]{1,0:T(8,128)(2,1)} collective-permute-done((bf16[320,256]{1,0:T(8,128)(2,1)}, bf16[320,256]{1,0:T(8,128)(2,1)}, u32[]{:S(2)}, u32[]{:S(2)}) %collective-permute-start) | collective-permute-done | bytes 163872 | tf_op jit(solution)/shard_map/ppermute | solution.py:30
  32.4 1.9 %collective-permute-start.2 = (bf16[320,256]{1,0:T(8,128)(2,1)}, bf16[320,256]{1,0:T(8,128)(2,1)S(1)}, u32[]{:S(2)}, u32[]{:S(2)}) collective-permute-start(bf16[320,256]{1,0:T(8,128)(2,1)} %collective-permute-done), channel_id=1, source_target_pairs={{0,64},{64,128},{128,192},{192,256},{256,320},{320,384},{384,448},... | collective-permute-start | bytes 491528 | tf_op jit(solution)/shard_map/ppermute | solution.py:30
  34.3 5.1 %collective-permute-start.3 = (bf16[320,256]{1,0:T(8,128)(2,1)S(1)}, bf16[320,256]{1,0:T(8,128)(2,1)S(1)}, u32[]{:S(2)}, u32[]{:S(2)}) collective-permute-start(bf16[320,256]{1,0:T(8,128)(2,1)S(1)} %collective-permute-done.1), channel_id=1, source_target_pairs={{0,960},{64,0},{128,64},{192,128},{256,192},{320,256},{384,320},{4... | collective-permute-start | bytes 491528 | tf_op jit(solution)/shard_map/ppermute | solution.py:33
  39.4 1.6 constant_dynamic-update-slice_fusion.14
  41.7 1.9 %collective-permute-start.4 = (bf16[320,256]{1,0:T(8,128)(2,1)S(1)}, bf16[320,256]{1,0:T(8,128)(2,1)S(1)}, u32[]{:S(2)}, u32[]{:S(2)}) collective-permute-start(bf16[320,256]{1,0:T(8,128)(2,1)S(1)} %collective-permute-done.2), channel_id=1, source_target_pairs={{0,64},{64,128},{128,192},{192,256},{256,320},{320,384},{384,448},... | collective-permute-start | bytes 491528 | tf_op jit(solution)/shard_map/ppermute | solution.py:30
  43.6 5.1 %collective-permute-start.5 = (bf16[320,256]{1,0:T(8,128)(2,1)S(1)}, bf16[320,256]{1,0:T(8,128)(2,1)S(1)}, u32[]{:S(2)}, u32[]{:S(2)}) collective-permute-start(bf16[320,256]{1,0:T(8,128)(2,1)S(1)} %collective-permute-done.3), channel_id=1, source_target_pairs={{0,960},{64,0},{128,64},{192,128},{256,192},{320,256},{384,320},{4... | collective-permute-start | bytes 491528 | tf_op jit(solution)/shard_map/ppermute | solution.py:33
  48.8 0.7 constant_dynamic-update-slice_fusion.12
  50.1 1.9 %collective-permute-start.6 = (bf16[320,256]{1,0:T(8,128)(2,1)S(1)}, bf16[320,256]{1,0:T(8,128)(2,1)S(1)}, u32[]{:S(2)}, u32[]{:S(2)}) collective-permute-start(bf16[320,256]{1,0:T(8,128)(2,1)S(1)} %collective-permute-done.4), channel_id=1, source_target_pairs={{0,64},{64,128},{128,192},{192,256},{256,320},{320,384},{384,448},... | collective-permute-start | bytes 491528 | tf_op jit(solution)/shard_map/ppermute | solution.py:30
  52.0 5.1 %collective-permute-start.7 = (bf16[320,256]{1,0:T(8,128)(2,1)S(1)}, bf16[320,256]{1,0:T(8,128)(2,1)S(1)}, u32[]{:S(2)}, u32[]{:S(2)}) collective-permute-start(bf16[320,256]{1,0:T(8,128)(2,1)S(1)} %collective-permute-done.5), channel_id=1, source_target_pairs={{0,960},{64,0},{128,64},{192,128},{256,192},{320,256},{384,320},{4... | collective-permute-start | bytes 491528 | tf_op jit(solution)/shard_map/ppermute | solution.py:33
  57.2 0.7 constant_dynamic-update-slice_fusion.10
  57.9 0.7 constant_dynamic-update-slice_fusion.9
  58.5 1.9 %collective-permute-start.8 = (bf16[320,256]{1,0:T(8,128)(2,1)S(1)}, bf16[320,256]{1,0:T(8,128)(2,1)S(1)}, u32[]{:S(2)}, u32[]{:S(2)}) collective-permute-start(bf16[320,256]{1,0:T(8,128)(2,1)S(1)} %collective-permute-done.6), channel_id=1, source_target_pairs={{0,64},{64,128},{128,192},{192,256},{256,320},{320,384},{384,448},... | collective-permute-start | bytes 491528 | tf_op jit(solution)/shard_map/ppermute | solution.py:30
  60.5 5.1 %collective-permute-start.9 = (bf16[320,256]{1,0:T(8,128)(2,1)S(1)}, bf16[320,256]{1,0:T(8,128)(2,1)S(1)}, u32[]{:S(2)}, u32[]{:S(2)}) collective-permute-start(bf16[320,256]{1,0:T(8,128)(2,1)S(1)} %collective-permute-done.7), channel_id=1, source_target_pairs={{0,960},{64,0},{128,64},{192,128},{256,192},{320,256},{384,320},{4... | collective-permute-start | bytes 491528 | tf_op jit(solution)/shard_map/ppermute | solution.py:33
  67.0 1.9 %collective-permute-start.10 = (bf16[320,256]{1,0:T(8,128)(2,1)S(1)}, bf16[320,256]{1,0:T(8,128)(2,1)S(1)}, u32[]{:S(2)}, u32[]{:S(2)}) collective-permute-start(bf16[320,256]{1,0:T(8,128)(2,1)S(1)} %collective-permute-done.8), channel_id=1, source_target_pairs={{0,64},{64,128},{128,192},{192,256},{256,320},{320,384},{384,448},... | collective-permute-start | bytes 491528 | tf_op jit(solution)/shard_map/ppermute | solution.py:30
  68.9 5.1 %collective-permute-start.11 = (bf16[320,256]{1,0:T(8,128)(2,1)S(1)}, bf16[320,256]{1,0:T(8,128)(2,1)S(1)}, u32[]{:S(2)}, u32[]{:S(2)}) collective-permute-start(bf16[320,256]{1,0:T(8,128)(2,1)S(1)} %collective-permute-done.9), channel_id=1, source_target_pairs={{0,960},{64,0},{128,64},{192,128},{256,192},{320,256},{384,320},{4... | collective-permute-start | bytes 491528 | tf_op jit(solution)/shard_map/ppermute | solution.py:33
  74.0 0.7 constant_dynamic-update-slice_fusion.6
  75.4 1.9 %collective-permute-start.12 = (bf16[320,256]{1,0:T(8,128)(2,1)S(1)}, bf16[320,256]{1,0:T(8,128)(2,1)S(1)}, u32[]{:S(2)}, u32[]{:S(2)}) collective-permute-start(bf16[320,256]{1,0:T(8,128)(2,1)S(1)} %collective-permute-done.10), channel_id=1, source_target_pairs={{0,64},{64,128},{128,192},{192,256},{256,320},{320,384},{384,448},... | collective-permute-start | bytes 491528 | tf_op jit(solution)/shard_map/ppermute | solution.py:30
  77.3 5.1 %collective-permute-start.13 = (bf16[320,256]{1,0:T(8,128)(2,1)S(1)}, bf16[320,256]{1,0:T(8,128)(2,1)S(1)}, u32[]{:S(2)}, u32[]{:S(2)}) collective-permute-start(bf16[320,256]{1,0:T(8,128)(2,1)S(1)} %collective-permute-done.11), channel_id=1, source_target_pairs={{0,960},{64,0},{128,64},{192,128},{256,192},{320,256},{384,320},{4... | collective-permute-start | bytes 491528 | tf_op jit(solution)/shard_map/ppermute | solution.py:33
  82.5 0.7 constant_dynamic-update-slice_fusion.4
  83.1 0.7 constant_dynamic-update-slice_fusion.3
  83.8 1.9 %collective-permute-start.14 = (bf16[320,256]{1,0:T(8,128)(2,1)S(1)}, bf16[320,256]{1,0:T(8,128)(2,1)S(1)}, u32[]{:S(2)}, u32[]{:S(2)}) collective-permute-start(bf16[320,256]{1,0:T(8,128)(2,1)S(1)} %collective-permute-done.12), channel_id=1, source_target_pairs={{0,64},{64,128},{128,192},{192,256},{256,320},{320,384},{384,448},... | collective-permute-start | bytes 491528 | tf_op jit(solution)/shard_map/ppermute | solution.py:30
  85.7 0.7 constant_dynamic-update-slice_fusion.2
  87.1 5.1 %collective-permute-done.14 = bf16[320,256]{1,0:T(8,128)(2,1)S(1)} collective-permute-done((bf16[320,256]{1,0:T(8,128)(2,1)S(1)}, bf16[320,256]{1,0:T(8,128)(2,1)S(1)}, u32[]{:S(2)}, u32[]{:S(2)}) %collective-permute-start.14) | collective-permute-done | bytes 163872 | tf_op jit(solution)/shard_map/ppermute | solution.py:30
  92.2 0.7 constant_dynamic-update-slice_fusion
  92.9 2.8 %fusion = (f32[320,256]{1,0:T(8,128)S(1)}, f32[320,256]{1,0:T(8,128)S(1)}) fusion(f32[320,256]{1,0:T(8,128)S(1)} %copy-done.4, f32[320,256]{1,0:T(8,128)S(1)} %copy-done.5, bf16[5120,320]{0,1:T(8,128)(2,1)S(1)} %copy-done, bf16[5120,256]{1,0:T(8,128)(2,1)} %constant_dynamic-update-slice_fusion), kind=kOutput, calls=%fused_computation.2 | convolution fusion | flops 839434240 | bytes 7208960 | tf_op jit(solution)/shard_map/dot_general | solution.py:42
  95.7 0.7 copy-done.1
  96.5 4.2 %fusion.1 = f32[256,5120]{0,1:T(8,128)} fusion(bf16[5120,320]{0,1:T(8,128)(2,1)S(1)} %copy-done, f32[320,256]{1,0:T(8,128)S(1)} %get-tuple-element.5, f32[320,256]{1,0:T(8,128)S(1)} %get-tuple-element.6), kind=kOutput, calls=%fused_computation.5 | convolution fusion | flops 839270400 | bytes 9175040 | tf_op jit(solution)/shard_map/dot_general | solution.py:46
  100.8 81.5 %reduce-scatter.2.cloned.1.call-done = f32[256,320]{0,1:T(8,128)} async-done(((f32[256,5120]{0,1:T(8,128)}), f32[256,320]{0,1:T(8,128)}) %reduce-scatter.2.cloned.1.call-update) | async-done | bytes 327696 | tf_op jit(solution)/shard_map/reduce_scatter | solution.py:49
  (32 shorter events, 4.2 us)
Async XLA Ops:
  7.2 85.8 %copy-start = (bf16[5120,320]{0,1:T(8,128)(2,1)S(1)}, bf16[5120,320]{0,1:T(8,128)(2,1)}, u32[]{:S(2)}) copy-start(bf16[5120,320]{0,1:T(8,128)(2,1)} %param.5) | copy-start | bytes 9830404
  7.2 175.1 %reduce-scatter.2.cloned.1.call-start = ((), (), s32[]{:S(2)}) async-start(), calls=%async_computation.1 | async-start | bytes 5570560 | tf_op jit(solution)/shard_map/reduce_scatter | solution.py:49
  7.2 1.7 copy-start.3
  9.6 22.7 %collective-permute-start = (bf16[320,256]{1,0:T(8,128)(2,1)}, bf16[320,256]{1,0:T(8,128)(2,1)}, u32[]{:S(2)}, u32[]{:S(2)}) collective-permute-start(bf16[320,256]{1,0:T(8,128)(2,1)} %get-tuple-element.4), channel_id=1, source_target_pairs={{0,64},{64,128},{128,192},{192,256},{256,320},{320,384},{384,448},... | collective-permute-start | bytes 491528 | tf_op jit(solution)/shard_map/ppermute | solution.py:30
  13.9 20.4 %collective-permute-start.1 = (bf16[320,256]{1,0:T(8,128)(2,1)}, bf16[320,256]{1,0:T(8,128)(2,1)S(1)}, u32[]{:S(2)}, u32[]{:S(2)}) collective-permute-start(bf16[320,256]{1,0:T(8,128)(2,1)} %get-tuple-element.4), channel_id=1, source_target_pairs={{0,960},{64,0},{128,64},{192,128},{256,192},{320,256},{384,320},{4... | collective-permute-start | bytes 491528 | tf_op jit(solution)/shard_map/ppermute | solution.py:33
  30.1 62.8 %copy-start.4 = (f32[320,256]{1,0:T(8,128)S(1)}, f32[320,256]{1,0:T(8,128)}, u32[]{:S(2)}) copy-start(f32[320,256]{1,0:T(8,128)} %param.7) | copy-start | bytes 983044
  30.1 62.8 %copy-start.5 = (f32[320,256]{1,0:T(8,128)S(1)}, f32[320,256]{1,0:T(8,128)}, u32[]{:S(2)}) copy-start(f32[320,256]{1,0:T(8,128)} %param.6) | copy-start | bytes 983044
  32.4 9.3 %collective-permute-start.2 = (bf16[320,256]{1,0:T(8,128)(2,1)}, bf16[320,256]{1,0:T(8,128)(2,1)S(1)}, u32[]{:S(2)}, u32[]{:S(2)}) collective-permute-start(bf16[320,256]{1,0:T(8,128)(2,1)} %collective-permute-done), channel_id=1, source_target_pairs={{0,64},{64,128},{128,192},{192,256},{256,320},{320,384},{384,448},... | collective-permute-start | bytes 491528 | tf_op jit(solution)/shard_map/ppermute | solution.py:30
  34.3 9.3 %collective-permute-start.3 = (bf16[320,256]{1,0:T(8,128)(2,1)S(1)}, bf16[320,256]{1,0:T(8,128)(2,1)S(1)}, u32[]{:S(2)}, u32[]{:S(2)}) collective-permute-start(bf16[320,256]{1,0:T(8,128)(2,1)S(1)} %collective-permute-done.1), channel_id=1, source_target_pairs={{0,960},{64,0},{128,64},{192,128},{256,192},{320,256},{384,320},{4... | collective-permute-start | bytes 491528 | tf_op jit(solution)/shard_map/ppermute | solution.py:33
  41.7 8.4 %collective-permute-start.4 = (bf16[320,256]{1,0:T(8,128)(2,1)S(1)}, bf16[320,256]{1,0:T(8,128)(2,1)S(1)}, u32[]{:S(2)}, u32[]{:S(2)}) collective-permute-start(bf16[320,256]{1,0:T(8,128)(2,1)S(1)} %collective-permute-done.2), channel_id=1, source_target_pairs={{0,64},{64,128},{128,192},{192,256},{256,320},{320,384},{384,448},... | collective-permute-start | bytes 491528 | tf_op jit(solution)/shard_map/ppermute | solution.py:30
  43.6 8.4 %collective-permute-start.5 = (bf16[320,256]{1,0:T(8,128)(2,1)S(1)}, bf16[320,256]{1,0:T(8,128)(2,1)S(1)}, u32[]{:S(2)}, u32[]{:S(2)}) collective-permute-start(bf16[320,256]{1,0:T(8,128)(2,1)S(1)} %collective-permute-done.3), channel_id=1, source_target_pairs={{0,960},{64,0},{128,64},{192,128},{256,192},{320,256},{384,320},{4... | collective-permute-start | bytes 491528 | tf_op jit(solution)/shard_map/ppermute | solution.py:33
  50.1 8.4 %collective-permute-start.6 = (bf16[320,256]{1,0:T(8,128)(2,1)S(1)}, bf16[320,256]{1,0:T(8,128)(2,1)S(1)}, u32[]{:S(2)}, u32[]{:S(2)}) collective-permute-start(bf16[320,256]{1,0:T(8,128)(2,1)S(1)} %collective-permute-done.4), channel_id=1, source_target_pairs={{0,64},{64,128},{128,192},{192,256},{256,320},{320,384},{384,448},... | collective-permute-start | bytes 491528 | tf_op jit(solution)/shard_map/ppermute | solution.py:30
  52.0 8.4 %collective-permute-start.7 = (bf16[320,256]{1,0:T(8,128)(2,1)S(1)}, bf16[320,256]{1,0:T(8,128)(2,1)S(1)}, u32[]{:S(2)}, u32[]{:S(2)}) collective-permute-start(bf16[320,256]{1,0:T(8,128)(2,1)S(1)} %collective-permute-done.5), channel_id=1, source_target_pairs={{0,960},{64,0},{128,64},{192,128},{256,192},{320,256},{384,320},{4... | collective-permute-start | bytes 491528 | tf_op jit(solution)/shard_map/ppermute | solution.py:33
  58.5 8.4 %collective-permute-start.8 = (bf16[320,256]{1,0:T(8,128)(2,1)S(1)}, bf16[320,256]{1,0:T(8,128)(2,1)S(1)}, u32[]{:S(2)}, u32[]{:S(2)}) collective-permute-start(bf16[320,256]{1,0:T(8,128)(2,1)S(1)} %collective-permute-done.6), channel_id=1, source_target_pairs={{0,64},{64,128},{128,192},{192,256},{256,320},{320,384},{384,448},... | collective-permute-start | bytes 491528 | tf_op jit(solution)/shard_map/ppermute | solution.py:30
  60.5 8.4 %collective-permute-start.9 = (bf16[320,256]{1,0:T(8,128)(2,1)S(1)}, bf16[320,256]{1,0:T(8,128)(2,1)S(1)}, u32[]{:S(2)}, u32[]{:S(2)}) collective-permute-start(bf16[320,256]{1,0:T(8,128)(2,1)S(1)} %collective-permute-done.7), channel_id=1, source_target_pairs={{0,960},{64,0},{128,64},{192,128},{256,192},{320,256},{384,320},{4... | collective-permute-start | bytes 491528 | tf_op jit(solution)/shard_map/ppermute | solution.py:33
  67.0 8.4 %collective-permute-start.10 = (bf16[320,256]{1,0:T(8,128)(2,1)S(1)}, bf16[320,256]{1,0:T(8,128)(2,1)S(1)}, u32[]{:S(2)}, u32[]{:S(2)}) collective-permute-start(bf16[320,256]{1,0:T(8,128)(2,1)S(1)} %collective-permute-done.8), channel_id=1, source_target_pairs={{0,64},{64,128},{128,192},{192,256},{256,320},{320,384},{384,448},... | collective-permute-start | bytes 491528 | tf_op jit(solution)/shard_map/ppermute | solution.py:30
  68.9 8.4 %collective-permute-start.11 = (bf16[320,256]{1,0:T(8,128)(2,1)S(1)}, bf16[320,256]{1,0:T(8,128)(2,1)S(1)}, u32[]{:S(2)}, u32[]{:S(2)}) collective-permute-start(bf16[320,256]{1,0:T(8,128)(2,1)S(1)} %collective-permute-done.9), channel_id=1, source_target_pairs={{0,960},{64,0},{128,64},{192,128},{256,192},{320,256},{384,320},{4... | collective-permute-start | bytes 491528 | tf_op jit(solution)/shard_map/ppermute | solution.py:33
  75.4 8.4 %collective-permute-start.12 = (bf16[320,256]{1,0:T(8,128)(2,1)S(1)}, bf16[320,256]{1,0:T(8,128)(2,1)S(1)}, u32[]{:S(2)}, u32[]{:S(2)}) collective-permute-start(bf16[320,256]{1,0:T(8,128)(2,1)S(1)} %collective-permute-done.10), channel_id=1, source_target_pairs={{0,64},{64,128},{128,192},{192,256},{256,320},{320,384},{384,448},... | collective-permute-start | bytes 491528 | tf_op jit(solution)/shard_map/ppermute | solution.py:30
  77.3 9.1 %collective-permute-start.13 = (bf16[320,256]{1,0:T(8,128)(2,1)S(1)}, bf16[320,256]{1,0:T(8,128)(2,1)S(1)}, u32[]{:S(2)}, u32[]{:S(2)}) collective-permute-start(bf16[320,256]{1,0:T(8,128)(2,1)S(1)} %collective-permute-done.11), channel_id=1, source_target_pairs={{0,960},{64,0},{128,64},{192,128},{256,192},{320,256},{384,320},{4... | collective-permute-start | bytes 491528 | tf_op jit(solution)/shard_map/ppermute | solution.py:33
  83.8 8.4 %collective-permute-start.14 = (bf16[320,256]{1,0:T(8,128)(2,1)S(1)}, bf16[320,256]{1,0:T(8,128)(2,1)S(1)}, u32[]{:S(2)}, u32[]{:S(2)}) collective-permute-start(bf16[320,256]{1,0:T(8,128)(2,1)S(1)} %collective-permute-done.12), channel_id=1, source_target_pairs={{0,64},{64,128},{128,192},{192,256},{256,320},{320,384},{384,448},... | collective-permute-start | bytes 491528 | tf_op jit(solution)/shard_map/ppermute | solution.py:30
  95.7 0.7 copy-start.1
  95.7 0.8 copy-start.2
Sparse Core Ops, SparseCore 0:
  100.9 81.3 reduce-scatter.1
